TPU v7x, 32 devices: a whole 2x2x4 slice. The times are simulated.
32 devices in a mesh: slab: 8 (over z, x), orient: 4 (over y, core).
Axes of the slice: x: 2, y: 2, z: 4, core: 2. Of those that a mesh axis runs over, the one named last changes fastest.
Arguments:
- tiles: bfloat16 [192, 1, 128, 128], P('slab'), may hold values from -8 to 8
- assigned_worker: int32 [192], P('slab'), may hold values from -1 to 7, as said below
- wedge_mask: int32 [128, 128], replicated, may hold values 0 or 1
- template_volume: float32 [64, 64, 64], replicated, may hold values from -6 to 6
- rotation_samples: int32 [64, 4096], P('orient', 'slab'), may hold values from 0 to 262143
Outputs:
- scores: bfloat16 [192, 128, 128], P('slab', 'orient')
Inputs may be any that keep to these rules, and one draw needn't show every extreme that they name: `assigned_worker`: the occupied slots of each slab index come first. Slab indices 2m and 2m+1 hold 24 occupied slots together, and some slab index has all 24 occupied. The occupied slots, taken in slot order over all slab indices, are dealt to the workers in turn, so every worker receives exactly 12 tiles and at most 3 from one slab index.
All inputs are finite; a program needn't handle non-finite values.
Results may differ from a plain program's by a relative error of at most 0.0085.
Values may be sent and summed in bfloat16 or wider, within the bound.
No kernel may reach another device: no remote copies, remote signals or barrier semaphores. Data moves between devices by JAX's collectives and lax.ppermute only.
A program may use at most 128 MiB of HBM per device.

v0:
```python
import math
import jax
import jax.numpy as jnp
from jax import lax
from jax.sharding import PartitionSpec as P


def partner(block, axis, bit):
    count = lax.axis_size(axis)
    route = []
    for low in range(count):
        high = low | 1 << bit
        if high != low and high < count:
            route += [(low, high), (high, low)]
    return lax.ppermute(block, axis, route)


def tables(length):
    counter = jnp.arange(length, dtype=jnp.int32)
    angles = (counter[:, None] * counter[None, :] % length).astype(jnp.float32) * (
        2.0 * math.pi / length
    )
    return (jnp.cos(angles).astype(jnp.bfloat16), jnp.sin(angles).astype(jnp.bfloat16))


def band_table(length, box_edge):
    counter = jnp.arange(length, dtype=jnp.int32)
    offsets = (counter[None, :] - counter[:, None]) % length
    return (offsets < box_edge).astype(jnp.float32)


def right_mul(values, table):
    return jnp.einsum("...ab,bc->...ac", values, table, preferred_element_type=jnp.float32)


def left_mul(table, values):
    return jnp.einsum("ka,...ab->...kb", table, values, preferred_element_type=jnp.float32)


def forward_two(values, cosine_table, sine_table):
    first_real = right_mul(values, cosine_table).astype(jnp.bfloat16)
    first_imag = (-right_mul(values, sine_table)).astype(jnp.bfloat16)
    second_real = (left_mul(cosine_table, first_real) + left_mul(sine_table, first_imag)).astype(
        jnp.bfloat16
    )
    second_imag = (left_mul(cosine_table, first_imag) - left_mul(sine_table, first_real)).astype(
        jnp.bfloat16
    )
    return (second_real, second_imag)


def inverse_real(real_part, imag_part, cosine_table, sine_table):
    length = real_part.shape[-1]
    first_real = (right_mul(real_part, cosine_table) - right_mul(imag_part, sine_table)).astype(
        jnp.bfloat16
    )
    first_imag = (right_mul(imag_part, cosine_table) + right_mul(real_part, sine_table)).astype(
        jnp.bfloat16
    )
    return (left_mul(cosine_table, first_real) - left_mul(sine_table, first_imag)) * (
        1.0 / (length * length)
    )


def filtered(values, wedge_weight, cosine_table, sine_table):
    spec_real, spec_imag = forward_two(values, cosine_table, sine_table)
    return inverse_real(
        spec_real * wedge_weight, spec_imag * wedge_weight, cosine_table, sine_table
    ).astype(jnp.bfloat16)


def pick_rows(chosen, source):
    counter = jnp.arange(source.shape[0], dtype=jnp.int32)
    selector = (chosen[:, None] == counter[None, :]).astype(source.dtype)
    flat = source.reshape(source.shape[0], -1)
    picked = jnp.dot(selector, flat, preferred_element_type=jnp.float32).astype(source.dtype)
    return picked.reshape((chosen.shape[0],) + source.shape[1:])


def make_templates(
    template_volume, rotation_samples, box_edge, planes, tile_len, cosine_table, sine_table
):
    count = rotation_samples.shape[0]
    sampled_part = jnp.take(template_volume.reshape(-1), rotation_samples, axis=0).astype(
        jnp.bfloat16
    )
    sampled = lax.all_gather(sampled_part, "slab", axis=1, tiled=True)
    sampled = sampled.reshape(count, planes, box_edge, box_edge)
    padded = jnp.pad(sampled, ((0, 0), (0, 0), (0, tile_len - box_edge), (0, tile_len - box_edge)))
    template_norm = jnp.sqrt(
        jnp.sum(jnp.square(sampled.astype(jnp.float32)), axis=(1, 2, 3)) + 1e-05
    )
    spec_real, spec_imag = forward_two(padded, cosine_table, sine_table)
    return (spec_real, spec_imag, template_norm)


def score_tiles(
    slab_field, templ_real, templ_imag, template_norm, cosine_table, sine_table, band_sum, box_edge
):
    planes = slab_field.shape[1]
    field_real, field_imag = forward_two(slab_field, cosine_table, sine_table)
    left_real = field_real.astype(jnp.float32)[:, None]
    left_imag = field_imag.astype(jnp.float32)[:, None]
    right_real = templ_real.astype(jnp.float32)[None]
    right_imag = templ_imag.astype(jnp.float32)[None]
    prod_real = jnp.sum(left_real * right_real + left_imag * right_imag, axis=2).astype(
        jnp.bfloat16
    )
    prod_imag = jnp.sum(left_imag * right_real - left_real * right_imag, axis=2).astype(
        jnp.bfloat16
    )
    correlation = inverse_real(prod_real, prod_imag, cosine_table, sine_table)
    energy = jnp.sum(jnp.square(slab_field.astype(jnp.float32)), axis=1)
    summed = jnp.einsum(
        "ka,nab,lb->nkl", band_sum, energy, band_sum, precision=lax.Precision.HIGHEST
    )
    local_rms = jnp.sqrt(summed / (box_edge * box_edge * planes) + 1e-05)
    ratio = correlation / (local_rms[:, None] * template_norm[None, :, None, None])
    return jnp.max(ratio, axis=1)


def orient_max(best):
    groups = lax.axis_size("orient")
    parts = lax.all_to_all(best, "orient", split_axis=1, concat_axis=0, tiled=True)
    stacked = parts.reshape(groups, best.shape[0], parts.shape[1], parts.shape[2])
    return jnp.max(stacked, axis=0)


def per_device(tiles, assigned_worker, wedge_mask, template_volume, rotation_samples):
    tile_len = tiles.shape[-1]
    planes = tiles.shape[1]
    home_slots = tiles.shape[0]
    work_slots = home_slots // 2
    box_edge = template_volume.shape[0]
    cosine_table, sine_table = tables(tile_len)
    band_sum = band_table(tile_len, box_edge)
    wedge_weight = wedge_mask.astype(jnp.bfloat16)
    templ_real, templ_imag, template_norm = make_templates(
        template_volume, rotation_samples, box_edge, planes, tile_len, cosine_table, sine_table
    )
    occupied = assigned_worker >= 0
    own_count = jnp.sum(occupied.astype(jnp.int32))
    partner_tiles = partner(tiles[work_slots:], "slab", 0)
    counter = jnp.arange(work_slots, dtype=jnp.int32)
    keep_own = (counter < own_count)[:, None, None, None]
    moved_in = pick_rows(counter - own_count, partner_tiles)
    gathered = jnp.where(keep_own, tiles[:work_slots], moved_in)
    slab_field = filtered(gathered, wedge_weight, cosine_table, sine_table)
    best = score_tiles(
        slab_field,
        templ_real,
        templ_imag,
        template_norm,
        cosine_table,
        sine_table,
        band_sum,
        box_edge,
    )
    best_rows = orient_max(best.astype(jnp.bfloat16))
    outgoing = pick_rows(counter + own_count, best_rows)
    returned = partner(outgoing, "slab", 0)
    result = jnp.concatenate([best_rows, returned], axis=0)
    return jnp.where(occupied[:, None, None], result, jnp.zeros_like(result))


def solution(mesh):
    return jax.shard_map(
        per_device,
        mesh=mesh,
        in_specs=(P("slab", None, None, None), P("slab"), P(), P(), P("orient", "slab")),
        out_specs=P("slab", "orient", None),
        check_vma=False,
    )
```

profile of v0, /device:TPU:0, one launch (start us, length us, event | category | flops | bytes accessed | tf_op | source)
XLA Modules:
  0.0 180.5 jit_solution(15834255213761315557)
XLA Ops:
  0.0 1.8 slice.7
  1.8 2.9 %collective-permute-start = (bf16[12,1,128,128]{3,2,1,0:T(8,128)(2,1)}, bf16[12,1,128,128]{3,2,1,0:T(8,128)(2,1)}, u32[]{:S(2)}, u32[]{:S(2)}) collective-permute-start(bf16[12,1,128,128]{3,2,1,0:T(8,128)(2,1)} %slice.7), channel_id=1, source_target_pairs={{0,4},{4,0},{8,12},{12,8},{16,20},{20,16},{24,28},{28,24},{1,5},{5... | collective-permute-start | bytes 1179656 | tf_op jit(solution)/shard_map/ppermute | solution.py:15
  4.7 1.9 %reshape.192 = bf16[262144]{0:T(1024)(128)(2,1)S(1)} reshape(f32[64,64,64]{2,1,0:T(8,128)} %param.8) | data formatting | bytes 1572864 | tf_op jit(solution)/shard_map/reshape | solution.py:84
  7.4 50.7 %gather_fusion = bf16[8192]{0:T(1024)(128)(2,1)S(1)} fusion(bf16[262144]{0:T(1024)(128)(2,1)S(1)} %reshape.192, s32[8192]{0:T(1024)S(1)} %broadcast_clamp_fusion), kind=kCustom, calls=%fused_computation | custom fusion | bytes 65536 | tf_op jit(solution)/shard_map/jit(_take)/gather | solution.py:84
  58.2 30.9 %all_gather.3 = bf16[16,4096]{1,0:T(8,128)(2,1)S(1)} all-gather(bf16[16,512]{1,0:T(8,128)(2,1)S(1)} %select_convert_fusion), channel_id=1, replica_groups=mesh['slab'=8,'orient'=4] {'slab'}, dimensions={1}, use_global_device_ids=true | all-gather | bytes 147456 | tf_op jit(solution)/shard_map/all_gather | solution.py:87
  97.3 1.5 convolution_convert_fusion.4
  98.8 1.5 fusion.29
  103.8 1.4 fusion.113
  105.1 2.9 %fusion.50 = f32[12,128,128]{2,1,0:T(8,128)} fusion(f32[12,128,128]{2,1,0:T(8,128)} %fusion.118, bf16[12,128,128]{1,2,0:T(8,128)(2,1)S(1)} %fusion.56), kind=kOutput, calls=%fused_computation.74 | convolution fusion | flops 101548032 | bytes 1966080 | tf_op jit(solution)/shard_map/ka,...ab->...kb/dot_general | solution.py:37
  108.0 2.2 %fusion.34 = bf16[12,128,128]{2,1,0:T(8,128)(2,1)S(1)} fusion(f32[12,128,128]{2,1,0:T(8,128)} %fusion.50, f32[12,128,128]{2,1,0:T(8,128)} %fusion.113, bf16[12,128,128]{1,2,0:T(8,128)(2,1)S(1)} %fusion.54), kind=kOutput, calls=%fused_computation.56 | convolution fusion | flops 102137856 | bytes 2359296 | tf_op jit(solution)/shard_map/ka,...ab->...kb/dot_general | solution.py:37
  111.2 1.5 fusion.57
  113.2 1.4 fusion.110
  114.6 1.4 fusion.46
  116.0 1.4 copy.134
  117.4 2.5 %fusion.49 = f32[12,128,128]{1,2,0:T(8,128)} fusion(f32[12,128,128]{2,1,0:T(8,128)} %fusion.110, bf16[12,128,128]{2,1,0:T(8,128)(2,1)S(1)} %fusion.35), kind=kOutput, calls=%fused_computation.73 | convolution fusion | flops 51167232 | bytes 1966080 | tf_op jit(solution)/shard_map/ka,...ab->...kb/dot_general | solution.py:37
  119.9 2.3 %copy.128 = f32[12,128,128]{2,1,0:T(8,128)} copy(f32[12,128,128]{1,2,0:T(8,128)} %fusion.49) | data formatting | bytes 1572864 | tf_op jit(solution)/shard_map/mul | solution.py:106
  122.2 6.9 %fusion.2 = f32[12,16,128,128]{3,2,1,0:T(8,128)} fusion(f32[16,128,128]{2,1,0:T(8,128)S(1)} %copy.137, f32[12,128,128]{2,1,0:T(8,128)S(1)} %copy.134, f32[16,128,128]{2,1,0:T(8,128)S(1)} %copy.131, f32[12,128,128]{2,1,0:T(8,128)} %copy.128), kind=kOutput, calls=%fused_computation.9 | convolution fusion | flops 818135040 | bytes 16252928 | tf_op jit(solution)/shard_map/...ab,bc->...ac/dot_general | solution.py:33
  129.1 5.8 %fusion.1 = f32[12,16,128,128]{3,2,1,0:T(8,128)} fusion(f32[16,128,128]{2,1,0:T(8,128)S(1)} %copy.137, f32[12,128,128]{2,1,0:T(8,128)S(1)} %copy.134, f32[16,128,128]{2,1,0:T(8,128)S(1)} %copy.131, f32[12,128,128]{2,1,0:T(8,128)S(1)} %copy-done), kind=kOutput, calls=%fused_computation.8 | convolution fusion | flops 818135040 | bytes 16252928 | tf_op jit(solution)/shard_map/...ab,bc->...ac/dot_general | solution.py:33
  134.9 10.1 %fusion.5 = f32[12,16,128,128]{3,2,1,0:T(8,128)} fusion(f32[12,16,128,128]{3,2,1,0:T(8,128)} %fusion.2, f32[16,128,128]{2,1,0:T(8,128)S(1)} %copy.137, f32[12,128,128]{2,1,0:T(8,128)S(1)} %copy.134, f32[16,128,128]{2,1,0:T(8,128)S(1)} %copy.131, f32[12,128,128]{2,1,0:T(8,128)} %copy.128), kind=kOutput, calls=%fused_computation.12 | convolution fusion | flops 1629978624 | bytes 28835840 | tf_op jit(solution)/shard_map/ka,...ab->...kb/dot_general | solution.py:37
  144.9 2.7 %fusion.27 = f32[12,128,128]{2,1,0:T(8,128)} fusion(f32[12,128,128]{1,2,0:T(8,128)} %fusion.57), kind=kOutput, calls=%fused_computation.40 | convolution fusion | flops 302596096 | bytes 1572864 | tf_op jit(solution)/shard_map/ka,nab,lb->nkl/dot_general | solution.py:114
  147.6 2.3 %copy.141 = f32[12,128,128]{1,2,0:T(8,128)} copy(f32[12,128,128]{2,1,0:T(8,128)} %fusion.27) | data formatting | bytes 1572864 | tf_op jit(solution)/shard_map/sqrt | solution.py:117
  150.0 12.2 %fusion = bf16[12,128,128]{1,2,0:T(8,128)(2,1)S(1)} fusion(f32[12,16,128,128]{3,2,1,0:T(8,128)} %fusion.5, f32[16]{0:T(128)S(1)} %add_sqrt_fusion, f32[12,128,128]{1,2,0:T(8,128)} %copy.141, f32[12,16,128,128]{3,2,1,0:T(8,128)} %fusion.1, f32[16,128,128]{2,1,0:T(8,128)S(1)} %copy.137, f32[12,128,128]{2,1,0:T(8,128)S(1)} %copy.134, ...), kind=kOutput, calls=%fused_computation.7 | convolution fusion | flops 1645510656 | bytes 30015552 | tf_op jit(solution)/shard_map/ka,...ab->...kb/dot_general | solution.py:37
  162.6 11.5 %all_to_all.12 = bf16[12,128,128]{2,0,1:T(8,128)(2,1)S(1)} all-to-all(bf16[12,128,128]{2,0,1:T(8,128)(2,1)S(1)} %copy.142), channel_id=1, replica_groups=mesh['slab'=8,'orient'=4] {'orient'}, dimensions={1} | all-to-all | bytes 786432 | tf_op jit(solution)/shard_map/all_to_all | solution.py:124
  175.2 4.4 %collective-permute-done.1 = bf16[12,32,128]{2,0,1:T(8,128)(2,1)S(1)} collective-permute-done((bf16[12,32,128]{2,0,1:T(8,128)(2,1)S(1)}, bf16[12,32,128]{2,0,1:T(8,128)(2,1)S(1)}, u32[]{:S(2)}, u32[]{:S(2)}) %collective-permute-start.1) | collective-permute-done | bytes 98336 | tf_op jit(solution)/shard_map/ppermute | solution.py:15
  (55 shorter events, 16.2 us)
Async XLA Ops:
  0.0 58.1 %copy-start.1 = (s32[16,512]{1,0:T(8,128)S(1)}, s32[16,512]{1,0:T(8,128)}, u32[]{:S(2)}) copy-start(s32[16,512]{1,0:T(8,128)} %param.9) | copy-start | bytes 98308
  1.8 93.7 %collective-permute-start = (bf16[12,1,128,128]{3,2,1,0:T(8,128)(2,1)}, bf16[12,1,128,128]{3,2,1,0:T(8,128)(2,1)}, u32[]{:S(2)}, u32[]{:S(2)}) collective-permute-start(bf16[12,1,128,128]{3,2,1,0:T(8,128)(2,1)} %slice.7), channel_id=1, source_target_pairs={{0,4},{4,0},{8,12},{12,8},{16,20},{20,16},{24,28},{28,24},{1,5},{5... | collective-permute-start | bytes 1179656 | tf_op jit(solution)/shard_map/ppermute | solution.py:15
  7.3 84.6 %copy-start.3 = (s32[24]{0:T(128)S(1)}, s32[24]{0:T(128)}, u32[]{:S(2)}) copy-start(s32[24]{0:T(128)} %param.6) | copy-start | bytes 292
  7.4 87.4 %copy-start.2 = (s32[128,128]{1,0:T(8,128)S(1)}, s32[128,128]{1,0:T(8,128)}, u32[]{:S(2)}) copy-start(s32[128,128]{1,0:T(8,128)} %param.7) | copy-start | bytes 196612
  122.2 6.9 %copy-start = (f32[12,128,128]{2,1,0:T(8,128)S(1)}, f32[12,128,128]{2,1,0:T(8,128)}, u32[]{:S(2)}) copy-start(f32[12,128,128]{2,1,0:T(8,128)} %copy.128) | copy-start | bytes 2359300
  174.6 5.0 %collective-permute-start.1 = (bf16[12,32,128]{2,0,1:T(8,128)(2,1)S(1)}, bf16[12,32,128]{2,0,1:T(8,128)(2,1)S(1)}, u32[]{:S(2)}, u32[]{:S(2)}) collective-permute-start(bf16[12,32,128]{2,0,1:T(8,128)(2,1)S(1)} %copy.144), channel_id=1, source_target_pairs={{0,4},{4,0},{8,12},{12,8},{16,20},{20,16},{24,28},{28,24},{1,5},{5... | collective-permute-start | bytes 294920 | tf_op jit(solution)/shard_map/ppermute | solution.py:15
where the time goes:
time: 181 us; the launch traced here: 180 us
  local copies, waits for them, and re-layouts  64.2 us (35%)
  matrix products  62.5 us (35%)
  blocking collectives  42.3 us (23%)
  waiting for transfers between devices  4.44 us (2%)
  starting transfers between devices  3.53 us (2%)
  other arithmetic  3.09 us (2%)
    gather x2, local copies, waits for them, and re-layouts, make_templates(): jnp.take(template_volume.reshape(-1), rotation_samples, axis=0)  50.7 us
    dot_general x16, matrix products, left_mul(): jnp.einsum('ka,...ab->...kb', table, values, preferred_element_type=jnp.f...  37.3 us
    all_gather x1, blocking collectives, make_templates(): sampled = lax.all_gather(sampled_part, 'slab', axis=1, tiled=True)  30.9 us
    dot_general x10, matrix products, right_mul(): jnp.einsum('...ab,bc->...ac', values, table, preferred_element_type=jnp.f...  20.4 us
    all_to_all x1, blocking collectives, orient_max(): lax.all_to_all(best, 'orient', split_axis=1, concat_axis=0, tiled=True)  11.5 us
    ppermute x2, waiting for transfers between devices, partner(): return lax.ppermute(block, axis, route)  4.44 us
    dot_general x2, matrix products, score_tiles(): jnp.einsum('ka,nab,lb->nkl', band_sum, energy, band_sum, precision=lax.Pr...  4.21 us
  transfers between devices with their start and end apart: 2, of which 1 were waited for; matrix products, arithmetic and copies ran while one was open for 33% of the time, Pallas kernels for 0%

commit v1 on v0

--- a/solution.py
+++ b/solution.py
@@ -84,7 +84,12 @@
     sampled_part = jnp.take(template_volume.reshape(-1), rotation_samples, axis=0).astype(
         jnp.bfloat16
     )
-    sampled = lax.all_gather(sampled_part, "slab", axis=1, tiled=True)
+    ring = [sampled_part]
+    for hop in range(7):
+        ring.append(lax.ppermute(ring[-1], "slab", [(dev, (dev + 1) % 8) for dev in range(8)]))
+    sampled = jnp.roll(
+        jnp.concatenate(ring[::-1], axis=1), (lax.axis_index("slab") + 1) * ring[0].shape[1], axis=1
+    )
     sampled = sampled.reshape(count, planes, box_edge, box_edge)
     padded = jnp.pad(sampled, ((0, 0), (0, 0), (0, tile_len - box_edge), (0, tile_len - box_edge)))
     template_norm = jnp.sqrt(

time: 181 us -> 193 us (1.066)
  waiting for transfers between devices: 4.44 us -> 44.5 us
  blocking collectives: 42.3 us -> 11.5 us
  matrix products: 62.5 us -> 65.4 us
    ppermute x0 -> x7, waiting for transfers between devices: none -> 39.5 us  [make_templates(): lax.ppermute(ring[-1], 'slab', [(dev, (dev + 1) % 8) for dev in range(8)])]
    all_gather x1 -> x0, blocking collectives: 30.9 us -> none  [make_templates(): sampled = lax.all_gather(sampled_part, 'slab', axis=1, tiled=True)]
    ppermute x2, starting transfers between devices: 3.53 us -> 0.07 us  [partner(): return lax.ppermute(block, axis, route)]
    ppermute x0 -> x7, starting transfers between devices: none -> 3.02 us  [make_templates(): lax.ppermute(ring[-1], 'slab', [(dev, (dev + 1) % 8) for dev in range(8)])]
    dot_general x16, matrix products: 37.3 us -> 39.8 us  [left_mul(): jnp.einsum('ka,...ab->...kb', table, values, preferred_element_type=jnp.f...]
  transfers between devices with their start and end apart: 2 -> 9, of which waited for: 1 -> 8; matrix products, arithmetic and copies ran while one was open for 33% -> 5% of each run, Pallas kernels for 0% -> 0%
where the time goes in v1:
time: 193 us; the launch traced here: 192 us
  matrix products  65.4 us (34%)
  local copies, waits for them, and re-layouts  63.2 us (33%)
  waiting for transfers between devices  44.5 us (23%)
  blocking collectives  11.5 us (6%)
  other arithmetic  4.21 us (2%)
  starting transfers between devices  3.09 us (2%)
    gather x2, local copies, waits for them, and re-layouts, make_templates(): jnp.take(template_volume.reshape(-1), rotation_samples, axis=0)  50.7 us
    dot_general x16, matrix products, left_mul(): jnp.einsum('ka,...ab->...kb', table, values, preferred_element_type=jnp.f...  39.8 us
    ppermute x7, waiting for transfers between devices, make_templates(): lax.ppermute(ring[-1], 'slab', [(dev, (dev + 1) % 8) for dev in range(8)])  39.5 us
    dot_general x10, matrix products, right_mul(): jnp.einsum('...ab,bc->...ac', values, table, preferred_element_type=jnp.f...  20.8 us
    all_to_all x1, blocking collectives, orient_max(): lax.all_to_all(best, 'orient', split_axis=1, concat_axis=0, tiled=True)  11.5 us
    ppermute x2, waiting for transfers between devices, partner(): return lax.ppermute(block, axis, route)  4.94 us
    dot_general x2, matrix products, score_tiles(): jnp.einsum('ka,nab,lb->nkl', band_sum, energy, band_sum, precision=lax.Pr...  4.18 us
  transfers between devices with their start and end apart: 9, of which 8 were waited for; matrix products, arithmetic and copies ran while one was open for 5% of the time, Pallas kernels for 0%

profile of v1, /device:TPU:0, one launch (start us, length us, event | category | flops | bytes accessed | tf_op | source)
XLA Modules:
  0.0 192.3 jit_solution(4574218473737472239)
XLA Ops:
  0.0 1.9 %reshape.192 = bf16[262144]{0:T(1024)(128)(2,1)S(1)} reshape(f32[64,64,64]{2,1,0:T(8,128)} %param.8) | data formatting | bytes 1572864 | tf_op jit(solution)/shard_map/reshape | solution.py:84
  2.8 50.7 %gather_fusion = bf16[8192]{0:T(1024)(128)(2,1)S(1)} fusion(bf16[262144]{0:T(1024)(128)(2,1)S(1)} %reshape.192, s32[8192]{0:T(1024)S(1)} %broadcast_clamp_fusion), kind=kCustom, calls=%fused_computation | custom fusion | bytes 65536 | tf_op jit(solution)/shard_map/jit(_take)/gather | solution.py:84
  53.5 3.0 %collective-permute-start.1 = (bf16[16,512]{1,0:T(8,128)(2,1)S(1)}, bf16[16,512]{1,0:T(8,128)(2,1)S(1)}, u32[]{:S(2)}, u32[]{:S(2)}) collective-permute-start(bf16[16,512]{1,0:T(8,128)(2,1)S(1)} %select_convert_fusion), channel_id=1, source_target_pairs={{0,4},{4,8},{8,12},{12,16},{16,20},{20,24},{24,28},{28,0},{1,5},{5... | collective-permute-start | bytes 49160 | tf_op jit(solution)/shard_map/ppermute | solution.py:89
  56.6 4.8 %collective-permute-done.1 = bf16[16,512]{1,0:T(8,128)(2,1)S(1)} collective-permute-done((bf16[16,512]{1,0:T(8,128)(2,1)S(1)}, bf16[16,512]{1,0:T(8,128)(2,1)S(1)}, u32[]{:S(2)}, u32[]{:S(2)}) %collective-permute-start.1) | collective-permute-done | bytes 16416 | tf_op jit(solution)/shard_map/ppermute | solution.py:89
  61.3 6.4 %collective-permute-done.2 = bf16[16,512]{1,0:T(8,128)(2,1)S(1)} collective-permute-done((bf16[16,512]{1,0:T(8,128)(2,1)S(1)}, bf16[16,512]{1,0:T(8,128)(2,1)S(1)}, u32[]{:S(2)}, u32[]{:S(2)}) %collective-permute-start.2) | collective-permute-done | bytes 16416 | tf_op jit(solution)/shard_map/ppermute | solution.py:89
  67.7 6.4 %collective-permute-done.3 = bf16[16,512]{1,0:T(8,128)(2,1)S(1)} collective-permute-done((bf16[16,512]{1,0:T(8,128)(2,1)S(1)}, bf16[16,512]{1,0:T(8,128)(2,1)S(1)}, u32[]{:S(2)}, u32[]{:S(2)}) %collective-permute-start.3) | collective-permute-done | bytes 16416 | tf_op jit(solution)/shard_map/ppermute | solution.py:89
  75.0 5.7 %collective-permute-done.4 = bf16[16,512]{1,0:T(8,128)(2,1)S(1)} collective-permute-done((bf16[16,512]{1,0:T(8,128)(2,1)S(1)}, bf16[16,512]{1,0:T(8,128)(2,1)S(1)}, u32[]{:S(2)}, u32[]{:S(2)}) %collective-permute-start.4) | collective-permute-done | bytes 16416 | tf_op jit(solution)/shard_map/ppermute | solution.py:89
  81.4 5.9 %collective-permute-done.5 = bf16[16,512]{1,0:T(8,128)(2,1)S(1)} collective-permute-done((bf16[16,512]{1,0:T(8,128)(2,1)S(1)}, bf16[16,512]{1,0:T(8,128)(2,1)S(1)}, u32[]{:S(2)}, u32[]{:S(2)}) %collective-permute-start.5) | collective-permute-done | bytes 16416 | tf_op jit(solution)/shard_map/ppermute | solution.py:89
  87.9 5.8 %collective-permute-done.6 = bf16[16,512]{1,0:T(8,128)(2,1)S(1)} collective-permute-done((bf16[16,512]{1,0:T(8,128)(2,1)S(1)}, bf16[16,512]{1,0:T(8,128)(2,1)S(1)}, u32[]{:S(2)}, u32[]{:S(2)}) %collective-permute-start.6) | collective-permute-done | bytes 16416 | tf_op jit(solution)/shard_map/ppermute | solution.py:89
  95.7 4.5 %collective-permute-done.7 = bf16[16,512]{1,0:T(8,128)(2,1)S(1)} collective-permute-done((bf16[16,512]{1,0:T(8,128)(2,1)S(1)}, bf16[16,512]{1,0:T(8,128)(2,1)S(1)}, u32[]{:S(2)}, u32[]{:S(2)}) %collective-permute-start.7) | collective-permute-done | bytes 16416 | tf_op jit(solution)/shard_map/ppermute | solution.py:89
  103.8 1.6 fusion.43
  116.4 2.8 %fusion.50 = f32[12,128,128]{2,1,0:T(8,128)} fusion(f32[12,128,128]{2,1,0:T(8,128)} %fusion.118, bf16[12,128,128]{1,2,0:T(8,128)(2,1)S(1)} %fusion.56), kind=kOutput, calls=%fused_computation.74 | convolution fusion | flops 101548032 | bytes 1966080 | tf_op jit(solution)/shard_map/ka,...ab->...kb/dot_general | solution.py:37
  119.3 2.2 %fusion.34 = bf16[12,128,128]{2,1,0:T(8,128)(2,1)S(1)} fusion(f32[12,128,128]{2,1,0:T(8,128)} %fusion.50, f32[12,128,128]{2,1,0:T(8,128)} %fusion.113, bf16[12,128,128]{1,2,0:T(8,128)(2,1)S(1)} %fusion.54), kind=kOutput, calls=%fused_computation.56 | convolution fusion | flops 102137856 | bytes 2359296 | tf_op jit(solution)/shard_map/ka,...ab->...kb/dot_general | solution.py:37
  127.3 1.6 copy.134
  128.8 2.5 %fusion.49 = f32[12,128,128]{1,2,0:T(8,128)} fusion(f32[12,128,128]{2,1,0:T(8,128)} %fusion.110, bf16[12,128,128]{2,1,0:T(8,128)(2,1)S(1)} %fusion.35), kind=kOutput, calls=%fused_computation.73 | convolution fusion | flops 51167232 | bytes 1966080 | tf_op jit(solution)/shard_map/ka,...ab->...kb/dot_general | solution.py:37
  131.4 2.3 %copy.128 = f32[12,128,128]{2,1,0:T(8,128)} copy(f32[12,128,128]{1,2,0:T(8,128)} %fusion.49) | data formatting | bytes 1572864 | tf_op jit(solution)/shard_map/mul | solution.py:111
  133.7 7.1 %fusion.2 = f32[12,16,128,128]{3,2,1,0:T(8,128)} fusion(f32[16,128,128]{2,1,0:T(8,128)S(1)} %copy.137, f32[12,128,128]{2,1,0:T(8,128)S(1)} %copy.134, f32[16,128,128]{2,1,0:T(8,128)S(1)} %copy.131, f32[12,128,128]{2,1,0:T(8,128)} %copy.128), kind=kOutput, calls=%fused_computation.9 | convolution fusion | flops 818135040 | bytes 16252928 | tf_op jit(solution)/shard_map/...ab,bc->...ac/dot_general | solution.py:33
  140.8 5.9 %fusion.1 = f32[12,16,128,128]{3,2,1,0:T(8,128)} fusion(f32[16,128,128]{2,1,0:T(8,128)S(1)} %copy.137, f32[12,128,128]{2,1,0:T(8,128)S(1)} %copy.134, f32[16,128,128]{2,1,0:T(8,128)S(1)} %copy.131, f32[12,128,128]{2,1,0:T(8,128)S(1)} %copy-done), kind=kOutput, calls=%fused_computation.8 | convolution fusion | flops 818135040 | bytes 16252928 | tf_op jit(solution)/shard_map/...ab,bc->...ac/dot_general | solution.py:33
  146.6 10.1 %fusion.5 = f32[12,16,128,128]{3,2,1,0:T(8,128)} fusion(f32[12,16,128,128]{3,2,1,0:T(8,128)} %fusion.2, f32[16,128,128]{2,1,0:T(8,128)S(1)} %copy.137, f32[12,128,128]{2,1,0:T(8,128)S(1)} %copy.134, f32[16,128,128]{2,1,0:T(8,128)S(1)} %copy.131, f32[12,128,128]{2,1,0:T(8,128)} %copy.128), kind=kOutput, calls=%fused_computation.12 | convolution fusion | flops 1629978624 | bytes 28835840 | tf_op jit(solution)/shard_map/ka,...ab->...kb/dot_general | solution.py:37
  156.7 2.7 %fusion.27 = f32[12,128,128]{2,1,0:T(8,128)} fusion(f32[12,128,128]{1,2,0:T(8,128)} %fusion.57), kind=kOutput, calls=%fused_computation.40 | convolution fusion | flops 302596096 | bytes 1572864 | tf_op jit(solution)/shard_map/ka,nab,lb->nkl/dot_general | solution.py:119
  159.4 2.3 %copy.141 = f32[12,128,128]{1,2,0:T(8,128)} copy(f32[12,128,128]{2,1,0:T(8,128)} %fusion.27) | data formatting | bytes 1572864 | tf_op jit(solution)/shard_map/sqrt | solution.py:122
  161.7 12.2 %fusion = bf16[12,128,128]{1,2,0:T(8,128)(2,1)S(1)} fusion(f32[12,16,128,128]{3,2,1,0:T(8,128)} %fusion.5, f32[16]{0:T(128)S(1)} %copy-done.6, f32[12,128,128]{1,2,0:T(8,128)} %copy.141, f32[12,16,128,128]{3,2,1,0:T(8,128)} %fusion.1, f32[16,128,128]{2,1,0:T(8,128)S(1)} %copy.137, f32[12,128,128]{2,1,0:T(8,128)S(1)} %copy.134, ...), kind=kOutput, calls=%fused_computation.7 | convolution fusion | flops 1645510656 | bytes 30015552 | tf_op jit(solution)/shard_map/ka,...ab->...kb/dot_general | solution.py:37
  174.4 11.5 %all_to_all.12 = bf16[12,128,128]{2,0,1:T(8,128)(2,1)S(1)} all-to-all(bf16[12,128,128]{2,0,1:T(8,128)(2,1)S(1)} %copy.142), channel_id=1, replica_groups=mesh['slab'=8,'orient'=4] {'orient'}, dimensions={1} | all-to-all | bytes 786432 | tf_op jit(solution)/shard_map/all_to_all | solution.py:129
  186.5 4.9 %collective-permute-done.8 = bf16[12,32,128]{2,0,1:T(8,128)(2,1)S(1)} collective-permute-done((bf16[12,32,128]{2,0,1:T(8,128)(2,1)S(1)}, bf16[12,32,128]{2,0,1:T(8,128)(2,1)S(1)}, u32[]{:S(2)}, u32[]{:S(2)}) %collective-permute-start.8) | collective-permute-done | bytes 98336 | tf_op jit(solution)/shard_map/ppermute | solution.py:15
  (90 shorter events, 27.0 us)
Async XLA Ops:
  0.0 53.5 %copy-start.3 = (s32[16,512]{1,0:T(8,128)S(1)}, s32[16,512]{1,0:T(8,128)}, u32[]{:S(2)}) copy-start(s32[16,512]{1,0:T(8,128)} %param.9) | copy-start | bytes 98308
  0.0 74.2 %copy-start.2 = (bf16[24,1,128,128]{3,2,1,0:T(8,128)(2,1)S(1)}, bf16[24,1,128,128]{3,2,1,0:T(8,128)(2,1)}, u32[]{:S(2)}) copy-start(bf16[24,1,128,128]{3,2,1,0:T(8,128)(2,1)} %param.5) | copy-start | bytes 2359300
  0.0 80.7 %copy-start.5 = (s32[24]{0:T(128)S(1)}, s32[24]{0:T(128)}, u32[]{:S(2)}) copy-start(s32[24]{0:T(128)} %param.6) | copy-start | bytes 292
  0.0 95.0 %copy-start.4 = (s32[128,128]{1,0:T(8,128)S(1)}, s32[128,128]{1,0:T(8,128)}, u32[]{:S(2)}) copy-start(s32[128,128]{1,0:T(8,128)} %param.7) | copy-start | bytes 196612
  53.5 7.8 %collective-permute-start.1 = (bf16[16,512]{1,0:T(8,128)(2,1)S(1)}, bf16[16,512]{1,0:T(8,128)(2,1)S(1)}, u32[]{:S(2)}, u32[]{:S(2)}) collective-permute-start(bf16[16,512]{1,0:T(8,128)(2,1)S(1)} %select_convert_fusion), channel_id=1, source_target_pairs={{0,4},{4,8},{8,12},{12,16},{16,20},{20,24},{24,28},{28,0},{1,5},{5... | collective-permute-start | bytes 49160 | tf_op jit(solution)/shard_map/ppermute | solution.py:89
  61.3 6.4 %collective-permute-start.2 = (bf16[16,512]{1,0:T(8,128)(2,1)S(1)}, bf16[16,512]{1,0:T(8,128)(2,1)S(1)}, u32[]{:S(2)}, u32[]{:S(2)}) collective-permute-start(bf16[16,512]{1,0:T(8,128)(2,1)S(1)} %collective-permute-done.1), channel_id=1, source_target_pairs={{0,4},{4,8},{8,12},{12,16},{16,20},{20,24},{24,28},{28,0},{1,5},{5... | collective-permute-start | bytes 49160 | tf_op jit(solution)/shard_map/ppermute | solution.py:89
  67.7 6.4 %collective-permute-start.3 = (bf16[16,512]{1,0:T(8,128)(2,1)S(1)}, bf16[16,512]{1,0:T(8,128)(2,1)S(1)}, u32[]{:S(2)}, u32[]{:S(2)}) collective-permute-start(bf16[16,512]{1,0:T(8,128)(2,1)S(1)} %collective-permute-done.2), channel_id=1, source_target_pairs={{0,4},{4,8},{8,12},{12,16},{16,20},{20,24},{24,28},{28,0},{1,5},{5... | collective-permute-start | bytes 49160 | tf_op jit(solution)/shard_map/ppermute | solution.py:89
  74.2 6.5 %collective-permute-start.4 = (bf16[16,512]{1,0:T(8,128)(2,1)S(1)}, bf16[16,512]{1,0:T(8,128)(2,1)S(1)}, u32[]{:S(2)}, u32[]{:S(2)}) collective-permute-start(bf16[16,512]{1,0:T(8,128)(2,1)S(1)} %collective-permute-done.3), channel_id=1, source_target_pairs={{0,4},{4,8},{8,12},{12,16},{16,20},{20,24},{24,28},{28,0},{1,5},{5... | collective-permute-start | bytes 49160 | tf_op jit(solution)/shard_map/ppermute | solution.py:89
  75.0 31.2 %collective-permute-start = (bf16[12,1,128,128]{3,2,1,0:T(8,128)(2,1)}, bf16[12,1,128,128]{3,2,1,0:T(8,128)(2,1)S(1)}, u32[]{:S(2)}, u32[]{:S(2)}) collective-permute-start(bf16[12,1,128,128]{3,2,1,0:T(8,128)(2,1)} %slice.7), channel_id=1, source_target_pairs={{0,4},{4,0},{8,12},{12,8},{16,20},{20,16},{24,28},{28,24},{1,5},{5... | collective-permute-start | bytes 1179656 | tf_op jit(solution)/shard_map/ppermute | solution.py:15
  80.7 6.6 %collective-permute-start.5 = (bf16[16,512]{1,0:T(8,128)(2,1)S(1)}, bf16[16,512]{1,0:T(8,128)(2,1)S(1)}, u32[]{:S(2)}, u32[]{:S(2)}) collective-permute-start(bf16[16,512]{1,0:T(8,128)(2,1)S(1)} %collective-permute-done.4), channel_id=1, source_target_pairs={{0,4},{4,8},{8,12},{12,16},{16,20},{20,24},{24,28},{28,0},{1,5},{5... | collective-permute-start | bytes 49160 | tf_op jit(solution)/shard_map/ppermute | solution.py:89
  87.3 6.4 %collective-permute-start.6 = (bf16[16,512]{1,0:T(8,128)(2,1)S(1)}, bf16[16,512]{1,0:T(8,128)(2,1)S(1)}, u32[]{:S(2)}, u32[]{:S(2)}) collective-permute-start(bf16[16,512]{1,0:T(8,128)(2,1)S(1)} %collective-permute-done.5), channel_id=1, source_target_pairs={{0,4},{4,8},{8,12},{12,16},{16,20},{20,24},{24,28},{28,0},{1,5},{5... | collective-permute-start | bytes 49160 | tf_op jit(solution)/shard_map/ppermute | solution.py:89
  93.7 6.4 %collective-permute-start.7 = (bf16[16,512]{1,0:T(8,128)(2,1)S(1)}, bf16[16,512]{1,0:T(8,128)(2,1)S(1)}, u32[]{:S(2)}, u32[]{:S(2)}) collective-permute-start(bf16[16,512]{1,0:T(8,128)(2,1)S(1)} %collective-permute-done.6), channel_id=1, source_target_pairs={{0,4},{4,8},{8,12},{12,16},{16,20},{20,24},{24,28},{28,0},{1,5},{5... | collective-permute-start | bytes 49160 | tf_op jit(solution)/shard_map/ppermute | solution.py:89
  101.3 1.6 copy-start.1
  133.7 7.1 %copy-start = (f32[12,128,128]{2,1,0:T(8,128)S(1)}, f32[12,128,128]{2,1,0:T(8,128)}, u32[]{:S(2)}) copy-start(f32[12,128,128]{2,1,0:T(8,128)} %copy.128) | copy-start | bytes 2359300
  146.6 15.1 %copy-start.6 = (f32[16]{0:T(128)S(1)}, f32[16]{0:T(128)}, u32[]{:S(2)}) copy-start(f32[16]{0:T(128)} %add_sqrt_fusion) | copy-start | bytes 196
  186.4 5.0 %collective-permute-start.8 = (bf16[12,32,128]{2,0,1:T(8,128)(2,1)S(1)}, bf16[12,32,128]{2,0,1:T(8,128)(2,1)S(1)}, u32[]{:S(2)}, u32[]{:S(2)}) collective-permute-start(bf16[12,32,128]{2,0,1:T(8,128)(2,1)S(1)} %copy.144), channel_id=1, source_target_pairs={{0,4},{4,0},{8,12},{12,8},{16,20},{20,16},{24,28},{28,24},{1,5},{5... | collective-permute-start | bytes 294920 | tf_op jit(solution)/shard_map/ppermute | solution.py:15
